TPU v7x, 256 devices: a whole 4x4x8 slice. The times are simulated.
256 devices in a mesh: band: 2 (over y_hi), domain: 128 (over y_lo, x, z, core).
Axes of the slice: x: 4, y: 4 (y_hi: 2, y_lo: 2; y = y_hi * 2 + y_lo), z: 8, core: 2. Of those that a mesh axis runs over, the one named last changes fastest.
Arguments:
- targets: float32 [4, 36864, 192], P('band', 'domain'), may hold values from -5 to 5
- partner_pool: bfloat16 [64, 36864, 192], P('band', 'domain'), may hold values from -5 to 5
- owners: int32 [2], replicated, may hold values from 0 to 1, as said below
- warm_start: bfloat16 [2, 8, 4, 36864, 192], P(None, None, 'band', 'domain'), may hold values from -6 to 6
Outputs:
- exchange: float32 [4, 36864, 192], P('band', 'domain')
Inputs may be any that keep to these rules, and one draw needn't show every extreme that they name: The 2 broadcast blocks have distinct owners.
All inputs are finite; a program needn't handle non-finite values.
Results may differ from a plain program's by a relative error of at most 0.0006.
Values may be sent and summed in bfloat16 or wider, within the bound.
No kernel may reach another device: no remote copies, remote signals or barrier semaphores. Data moves between devices by JAX's collectives and lax.ppermute only.
A program may use at most 192 MiB of HBM per device.

v0:
```python
import math
import jax
import jax.numpy as jnp
from jax import lax
from jax.sharding import PartitionSpec as P

ORB = 8
STEPS = 2
SWEEPS = 3
GX = 192
GY = 192
GZ = 192
coupling = 4.0 * math.pi


def spread(block, axis, owner):
    block = jnp.where(lax.axis_index(axis) == owner, block, jnp.zeros_like(block))
    return lax.psum(block, axis)


def padded(block, sides, width):
    for axis, dim in sides:
        count = lax.axis_size(axis)
        forward = [(i, i + 1) for i in range(count - 1)]
        forward.append((count - 1, 0))
        backward = [(target, source) for source, target in forward]
        low = lax.ppermute(
            lax.slice_in_dim(block, block.shape[dim] - width, None, axis=dim), axis, forward
        )
        high = lax.ppermute(lax.slice_in_dim(block, 0, width, axis=dim), axis, backward)
        block = jnp.concatenate([low, block, high], axis=dim)
    return block


def row_sweep(widened, source, first_row):
    row_count = source.shape[1]
    line = GY
    centre = widened[:, line : line + row_count]
    beside = widened[:, :row_count] + widened[:, 2 * line : 2 * line + row_count]
    column = (first_row + jnp.arange(row_count, dtype=jnp.int32)) % line
    at_end = (column == line - 1)[None, :, None]
    at_start = (column == 0)[None, :, None]
    upper = jnp.where(
        at_end, widened[:, 1 : row_count + 1], widened[:, line + 1 : line + row_count + 1]
    )
    lower = jnp.where(
        at_start,
        widened[:, 2 * line - 1 : 2 * line - 1 + row_count],
        widened[:, line - 1 : line - 1 + row_count],
    )
    beside = beside + upper + lower + jnp.roll(centre, 1, 2) + jnp.roll(centre, -1, 2)
    return (beside + coupling * source) / 6.0


def fetch_block(partner_pool, owners, block_index):
    own_block = partner_pool[block_index * ORB : (block_index + 1) * ORB]
    return spread(own_block, "band", owners[block_index]).astype(jnp.float32)


def pair_products(partner, targets):
    density = partner[:, None] * targets[None]
    return (density, jnp.sum(density, axis=(2, 3)))


def solve_block(partner, density, mean_value, warm_block, first_row):
    block_width = partner.shape[0]
    target_count = density.shape[1]
    pair_count = block_width * target_count
    planes = density.shape[2:]
    source = density.reshape((pair_count,) + planes) - mean_value.reshape(pair_count, 1, 1)
    potential = warm_block.reshape((pair_count,) + planes).astype(jnp.float32)
    for sweep_index in range(SWEEPS):
        widened = padded(potential.astype(jnp.bfloat16), (("domain", 1),), GY).astype(
            potential.dtype
        )
        potential = row_sweep(widened, source, first_row)
    potential = potential.reshape((block_width, target_count) + planes)
    return jnp.sum(potential * partner[:, None], axis=0)


def body(targets, partner_pool, owners, warm_start):
    row_count = targets.shape[1]
    first_row = lax.axis_index("domain") * row_count
    cell_count = GX * GY * GZ
    exchange = jnp.zeros(targets.shape, jnp.float32)
    for block_index in range(STEPS):
        partner = fetch_block(partner_pool, owners, block_index)
        density, local_sums = pair_products(partner, targets)
        totals = lax.psum(local_sums, "domain")
        exchange = exchange - solve_block(
            partner, density, totals / cell_count, warm_start[block_index], first_row
        )
    return exchange


def solution(mesh):
    return jax.shard_map(
        body,
        mesh=mesh,
        in_specs=(
            P("band", "domain", None),
            P("band", "domain", None),
            P(),
            P(None, None, "band", "domain", None),
        ),
        out_specs=P("band", "domain", None),
        check_vma=False,
    )
```

profile of v0, /device:TPU:8, one launch (start us, length us, event | category | flops | bytes accessed | tf_op | source)
XLA Modules:
  0.0 645.0 jit_solution(16177434050569279853)
XLA Ops:
  11.4 7.4 %collective-permute-start.1 = (bf16[16,192,192]{2,1,0:T(8,128)(2,1)}, bf16[16,192,192]{2,1,0:T(8,128)(2,1)}, u32[]{:S(2)}, u32[]{:S(2)}) collective-permute-start(bf16[16,192,192]{2,1,0:T(8,128)(2,1)} %get-tuple-element.46), channel_id=1, source_target_pairs={{1,0},{2,1},{3,2},{4,3},{5,4},{6,5},{7,6},{8,7},{9,8},{10,9},{11,1... | collective-permute-start | bytes 3538952 | tf_op jit(solution)/shard_map/ppermute | solution.py:30
  20.2 6.5 %collective-permute-start.7 = (bf16[16,192,192]{2,1,0:T(8,128)(2,1)S(1)}, bf16[16,192,192]{2,1,0:T(8,128)(2,1)}, u32[]{:S(2)}, u32[]{:S(2)}) collective-permute-start(bf16[16,192,192]{2,1,0:T(8,128)(2,1)S(1)} %get-tuple-element.52), channel_id=1, source_target_pairs={{1,0},{2,1},{3,2},{4,3},{5,4},{6,5},{7,6},{8,7},{9,8},{10,9},{11,1... | collective-permute-start | bytes 3538952 | tf_op jit(solution)/shard_map/ppermute | solution.py:30
  31.9 5.2 collective-permute-done
  37.2 4.5 maximum_convert_fusion
  45.2 8.9 %collective-permute-done.6 = bf16[16,192,192]{2,1,0:T(8,128)(2,1)} collective-permute-done((bf16[16,192,192]{2,1,0:T(8,128)(2,1)}, bf16[16,192,192]{2,1,0:T(8,128)(2,1)}, u32[]{:S(2)}, u32[]{:S(2)}) %collective-permute-start.6) | collective-permute-done | bytes 1179680 | tf_op jit(solution)/shard_map/ppermute | solution.py:27
  54.1 3.8 maximum_convert_fusion.3
  61.3 10.6 %fusion.51 = (f32[16,288,191]{2,1,0:T(8,128)}, f32[16,288,191]{2,1,0:T(8,128)}) fusion(f32[16,672,192]{2,1,0:T(8,128)} %copy-done.3), kind=kLoop, calls=%fused_computation.90 | loop fusion | bytes 14082048 | tf_op jit(solution)/shard_map/jit(_roll_static)/slice | solution.py:51
  71.9 5.4 fusion.57
  77.3 43.5 %all-reduce.4.cloned.1.call-done = (bf16[8,288,192]{2,1,0:T(8,128)(2,1)}, bf16[8,288,192]{2,1,0:T(8,128)(2,1)}) async-done(((bf16[8,288,192]{2,1,0:T(8,128)(2,1)}, bf16[8,288,192]{2,1,0:T(8,128)(2,1)}), (bf16[8,288,192]{2,1,0:T(8,128)(2,1)}, bf16[8,288,192]{2,1,0:T(8,128)(2,1)})) %all-reduce.4.cloned.1.call-update) | async-done | bytes 1769488 | tf_op jit(solution)/shard_map/psum | solution.py:18
  124.7 4.9 fusion.42
  129.6 285.4 %all-reduce = (f32[8,2]{1,0:T(8,128)S(1)}, f32[8,2]{1,0:T(8,128)S(1)}) all-reduce(f32[8,2]{1,0:T(8,128)S(1)} %get-tuple-element.6, f32[8,2]{1,0:T(8,128)S(1)} %get-tuple-element.5), channel_id=1, replica_groups=mesh['band'=2,'domain'=128] {'domain'}, use_global_device_ids=true, to_apply=%region_6.7 | all-reduce | flops 32 | bytes 256 | tf_op jit(solution)/shard_map/psum | solution.py:89
  415.1 18.2 %fusion.38 = bf16[16,288,192]{2,1,0:T(8,128)(2,1)S(1)} fusion(f32[16,672,192]{2,1,0:T(8,128)} %copy-done.3, f32[16,288,191]{2,1,0:T(8,128)} %get-tuple-element.20, f32[16,288,1]{2,1,0:T(8,128)} %get-tuple-element.22, f32[16,288,1]{2,1,0:T(8,128)} %get-tuple-element.21, f32[16,288,191]{2,1,0:T(8,128)} %get-tuple-element.19, ...), kind=kLoop, calls=%fused_computation.60 | loop fusion | flops 12386304 | bytes 33620608 | tf_op jit(solution)/shard_map/convert_element_type | solution.py:73
  435.6 6.0 collective-permute-start.3
  441.7 19.7 %fusion.18 = bf16[16,288,192]{2,1,0:T(8,128)(2,1)} fusion(f32[16,672,192]{2,1,0:T(8,128)} %copy-done.2, f32[16,288,191]{2,1,0:T(8,128)} %get-tuple-element.32, f32[16,288,1]{2,1,0:T(8,128)} %get-tuple-element.34, f32[16,288,1]{2,1,0:T(8,128)} %get-tuple-element.33, f32[16,288,191]{2,1,0:T(8,128)} %get-tuple-element.31, ...), kind=kLoop, calls=%fused_computation.31 | loop fusion | flops 12386304 | bytes 33620608 | tf_op jit(solution)/shard_map/convert_element_type | solution.py:73
  461.3 3.9 fusion.64
  465.2 6.2 collective-permute-start.9
  471.4 3.8 maximum_convert_fusion.1
  475.2 3.6 fusion.50
  478.8 5.3 fusion.49
  484.1 5.4 collective-permute-done.8
  493.0 5.8 fusion.55
  502.8 18.2 %fusion.31 = bf16[16,288,192]{2,1,0:T(8,128)(2,1)S(1)} fusion(f32[16,672,192]{2,1,0:T(8,128)} %copy-done.5, f32[16,288,191]{2,1,0:T(8,128)} %get-tuple-element.16, f32[16,288,1]{2,1,0:T(8,128)} %get-tuple-element.18, f32[16,288,1]{2,1,0:T(8,128)} %get-tuple-element.17, f32[16,288,191]{2,1,0:T(8,128)} %get-tuple-element.15, ...), kind=kLoop, calls=%fused_computation.50 | loop fusion | flops 12386304 | bytes 33620608 | tf_op jit(solution)/shard_map/convert_element_type | solution.py:73
  523.2 6.4 collective-permute-start.5
  529.6 19.5 %fusion.11 = bf16[16,288,192]{2,1,0:T(8,128)(2,1)} fusion(f32[16,672,192]{2,1,0:T(8,128)} %copy-done.4, f32[16,288,191]{2,1,0:T(8,128)} %get-tuple-element.28, f32[16,288,1]{2,1,0:T(8,128)} %get-tuple-element.30, f32[16,288,1]{2,1,0:T(8,128)} %get-tuple-element.29, f32[16,288,191]{2,1,0:T(8,128)} %get-tuple-element.27, ...), kind=kLoop, calls=%fused_computation.21 | loop fusion | flops 12386304 | bytes 33620608 | tf_op jit(solution)/shard_map/convert_element_type | solution.py:73
  549.1 3.9 fusion.63
  553.0 6.0 collective-permute-start.11
  559.0 3.8 maximum_convert_fusion.2
  566.1 5.3 fusion.47
  571.4 5.8 collective-permute-done.10
  580.6 5.8 fusion.53
  590.5 20.2 %fusion.24 = f32[16,288,192]{2,1,0:T(8,128)} fusion(f32[16,672,192]{2,1,0:T(8,128)} %copy-done, f32[16,288,191]{2,1,0:T(8,128)} %get-tuple-element.12, f32[16,288,1]{2,1,0:T(8,128)} %get-tuple-element.14, f32[16,288,1]{2,1,0:T(8,128)} %get-tuple-element.13, f32[16,288,191]{2,1,0:T(8,128)} %get-tuple-element.11, f32[8,2,288,192]{3,2,1,0:T(8,128)} %get-tuple-element.39, ...), kind=kLoop, calls=%fused_computation.40 | loop fusion | flops 11501568 | bytes 35390080 | tf_op jit(solution)/shard_map/div | solution.py:52
  613.7 20.0 %fusion.4 = f32[16,288,192]{2,1,0:T(8,128)} fusion(f32[16,672,192]{2,1,0:T(8,128)} %copy-done.1, f32[16,288,191]{2,1,0:T(8,128)} %get-tuple-element.24, f32[16,288,1]{2,1,0:T(8,128)} %get-tuple-element.26, f32[16,288,1]{2,1,0:T(8,128)} %get-tuple-element.25, f32[16,288,191]{2,1,0:T(8,128)} %get-tuple-element.23, f32[8,2,288,192]{3,2,1,0:T(8,128)} %get-tuple-element.40, ...), kind=kLoop, calls=%fused_computation.11 | loop fusion | flops 11501568 | bytes 35390080 | tf_op jit(solution)/shard_map/div | solution.py:52
  (72 shorter events, 50.8 us)
Async XLA Ops:
  6.5 114.3 %all-reduce.4.cloned.1.call-start = ((), (), s32[]{:S(2)}) async-start(), calls=%async_computation | async-start | bytes 4718592 | tf_op jit(solution)/shard_map/psum | solution.py:18
  9.2 11.0 %copy-start.8 = (bf16[1,8,2,288,192]{4,3,2,1,0:T(8,128)(2,1)}, bf16[1,8,2,288,192]{4,3,2,1,0:T(8,128)(2,1)S(1)}, u32[]{:S(2)}) copy-start(bf16[1,8,2,288,192]{4,3,2,1,0:T(8,128)(2,1)S(1)} %get-tuple-element.36) | copy-start | bytes 5308420
  9.2 11.0 %copy-start.9 = (bf16[1,8,2,288,192]{4,3,2,1,0:T(8,128)(2,1)}, bf16[1,8,2,288,192]{4,3,2,1,0:T(8,128)(2,1)S(1)}, u32[]{:S(2)}) copy-start(bf16[1,8,2,288,192]{4,3,2,1,0:T(8,128)(2,1)S(1)} %get-tuple-element.35) | copy-start | bytes 5308420
  11.4 15.3 %copy-start.15 = (s32[2]{0:T(128)S(1)}, s32[2]{0:T(128)}, u32[]{:S(2)}) copy-start(s32[2]{0:T(128)} %param.6) | copy-start | bytes 28
  11.4 25.8 %collective-permute-start = (bf16[16,192,192]{2,1,0:T(8,128)(2,1)}, bf16[16,192,192]{2,1,0:T(8,128)(2,1)}, u32[]{:S(2)}, u32[]{:S(2)}) collective-permute-start(bf16[16,192,192]{2,1,0:T(8,128)(2,1)} %get-tuple-element.45), channel_id=1, source_target_pairs={{0,1},{1,2},{2,3},{3,4},{4,5},{5,6},{6,7},{7,8},{8,9},{9,10},{10,1... | collective-permute-start | bytes 3538952 | tf_op jit(solution)/shard_map/ppermute | solution.py:27
  11.4 25.8 %collective-permute-start.1 = (bf16[16,192,192]{2,1,0:T(8,128)(2,1)}, bf16[16,192,192]{2,1,0:T(8,128)(2,1)}, u32[]{:S(2)}, u32[]{:S(2)}) collective-permute-start(bf16[16,192,192]{2,1,0:T(8,128)(2,1)} %get-tuple-element.46), channel_id=1, source_target_pairs={{1,0},{2,1},{3,2},{4,3},{5,4},{6,5},{7,6},{8,7},{9,8},{10,9},{11,1... | collective-permute-start | bytes 3538952 | tf_op jit(solution)/shard_map/ppermute | solution.py:30
  20.2 33.9 %collective-permute-start.6 = (bf16[16,192,192]{2,1,0:T(8,128)(2,1)}, bf16[16,192,192]{2,1,0:T(8,128)(2,1)}, u32[]{:S(2)}, u32[]{:S(2)}) collective-permute-start(bf16[16,192,192]{2,1,0:T(8,128)(2,1)} %get-tuple-element.51), channel_id=1, source_target_pairs={{0,1},{1,2},{2,3},{3,4},{4,5},{5,6},{6,7},{7,8},{8,9},{9,10},{10,1... | collective-permute-start | bytes 3538952 | tf_op jit(solution)/shard_map/ppermute | solution.py:27
  20.2 33.9 %collective-permute-start.7 = (bf16[16,192,192]{2,1,0:T(8,128)(2,1)S(1)}, bf16[16,192,192]{2,1,0:T(8,128)(2,1)}, u32[]{:S(2)}, u32[]{:S(2)}) collective-permute-start(bf16[16,192,192]{2,1,0:T(8,128)(2,1)S(1)} %get-tuple-element.52), channel_id=1, source_target_pairs={{1,0},{2,1},{3,2},{4,3},{5,4},{6,5},{7,6},{8,7},{9,8},{10,9},{11,1... | collective-permute-start | bytes 3538952 | tf_op jit(solution)/shard_map/ppermute | solution.py:30
  41.7 12.4 %copy-start.3 = (f32[16,672,192]{2,1,0:T(8,128)}, f32[16,672,192]{2,1,0:T(8,128)S(1)}, u32[]{:S(2)}) copy-start(f32[16,672,192]{2,1,0:T(8,128)S(1)} %maximum_convert_fusion) | copy-start | bytes 24772612
  57.9 14.0 %copy-start.2 = (f32[16,672,192]{2,1,0:T(8,128)}, f32[16,672,192]{2,1,0:T(8,128)S(1)}, u32[]{:S(2)}) copy-start(f32[16,672,192]{2,1,0:T(8,128)S(1)} %maximum_convert_fusion.3) | copy-start | bytes 24772612
  77.3 47.4 %copy-start.14 = (f32[2,288,192]{2,1,0:T(8,128)S(1)}, f32[2,288,192]{2,1,0:T(8,128)}, u32[]{:S(2)}) copy-start(f32[2,288,192]{2,1,0:T(8,128)} %param.4) | copy-start | bytes 1327108
  122.3 7.2 %copy-start.12 = (f32[8,288,192]{2,1,0:T(8,128)}, f32[8,288,192]{2,1,0:T(8,128)S(1)}, u32[]{:S(2)}) copy-start(f32[8,288,192]{2,1,0:T(8,128)S(1)} %convert_element_type.41) | copy-start | bytes 5308420
  124.7 4.9 copy-start.10
  433.3 28.0 %copy-start.6 = (bf16[16,288,192]{2,1,0:T(8,128)(2,1)}, bf16[16,288,192]{2,1,0:T(8,128)(2,1)S(1)}, u32[]{:S(2)}) copy-start(bf16[16,288,192]{2,1,0:T(8,128)(2,1)S(1)} %fusion.38) | copy-start | bytes 5308420
  435.5 35.9 %collective-permute-start.2 = (bf16[16,192,192]{2,1,0:T(8,128)(2,1)}, bf16[16,192,192]{2,1,0:T(8,128)(2,1)}, u32[]{:S(2)}, u32[]{:S(2)}) collective-permute-start(bf16[16,192,192]{2,1,0:T(8,128)(2,1)} %get-tuple-element.43), channel_id=1, source_target_pairs={{0,1},{1,2},{2,3},{3,4},{4,5},{5,6},{6,7},{7,8},{8,9},{9,10},{10,1... | collective-permute-start | bytes 3538952 | tf_op jit(solution)/shard_map/ppermute | solution.py:27
  435.6 35.8 %collective-permute-start.3 = (bf16[16,192,192]{2,1,0:T(8,128)(2,1)}, bf16[16,192,192]{2,1,0:T(8,128)(2,1)}, u32[]{:S(2)}, u32[]{:S(2)}) collective-permute-start(bf16[16,192,192]{2,1,0:T(8,128)(2,1)} %get-tuple-element.44), channel_id=1, source_target_pairs={{1,0},{2,1},{3,2},{4,3},{5,4},{6,5},{7,6},{8,7},{9,8},{10,9},{11,1... | collective-permute-start | bytes 3538952 | tf_op jit(solution)/shard_map/ppermute | solution.py:30
  465.2 24.3 %collective-permute-start.8 = (bf16[16,192,192]{2,1,0:T(8,128)(2,1)}, bf16[16,192,192]{2,1,0:T(8,128)(2,1)S(1)}, u32[]{:S(2)}, u32[]{:S(2)}) collective-permute-start(bf16[16,192,192]{2,1,0:T(8,128)(2,1)} %get-tuple-element.49), channel_id=1, source_target_pairs={{0,1},{1,2},{2,3},{3,4},{4,5},{5,6},{6,7},{7,8},{8,9},{9,10},{10,1... | collective-permute-start | bytes 3538952 | tf_op jit(solution)/shard_map/ppermute | solution.py:27
  465.2 24.4 %collective-permute-start.9 = (bf16[16,192,192]{2,1,0:T(8,128)(2,1)}, bf16[16,192,192]{2,1,0:T(8,128)(2,1)}, u32[]{:S(2)}, u32[]{:S(2)}) collective-permute-start(bf16[16,192,192]{2,1,0:T(8,128)(2,1)} %get-tuple-element.50), channel_id=1, source_target_pairs={{1,0},{2,1},{3,2},{4,3},{5,4},{6,5},{7,6},{8,7},{9,8},{10,9},{11,1... | collective-permute-start | bytes 3538952 | tf_op jit(solution)/shard_map/ppermute | solution.py:30
  475.2 9.0 %copy-start.5 = (f32[16,672,192]{2,1,0:T(8,128)}, f32[16,672,192]{2,1,0:T(8,128)S(1)}, u32[]{:S(2)}) copy-start(f32[16,672,192]{2,1,0:T(8,128)S(1)} %maximum_convert_fusion.1) | copy-start | bytes 24772612
  492.9 6.9 %copy-start.4 = (f32[16,672,192]{2,1,0:T(8,128)}, f32[16,672,192]{2,1,0:T(8,128)S(1)}, u32[]{:S(2)}) copy-start(f32[16,672,192]{2,1,0:T(8,128)S(1)} %maximum_convert_fusion.4) | copy-start | bytes 24772612
  521.1 28.0 %copy-start.7 = (bf16[16,288,192]{2,1,0:T(8,128)(2,1)}, bf16[16,288,192]{2,1,0:T(8,128)(2,1)S(1)}, u32[]{:S(2)}) copy-start(bf16[16,288,192]{2,1,0:T(8,128)(2,1)S(1)} %fusion.31) | copy-start | bytes 5308420
  523.2 35.8 %collective-permute-start.4 = (bf16[16,192,192]{2,1,0:T(8,128)(2,1)}, bf16[16,192,192]{2,1,0:T(8,128)(2,1)}, u32[]{:S(2)}, u32[]{:S(2)}) collective-permute-start(bf16[16,192,192]{2,1,0:T(8,128)(2,1)} %get-tuple-element.41), channel_id=1, source_target_pairs={{0,1},{1,2},{2,3},{3,4},{4,5},{5,6},{6,7},{7,8},{8,9},{9,10},{10,1... | collective-permute-start | bytes 3538952 | tf_op jit(solution)/shard_map/ppermute | solution.py:27
  523.2 35.8 %collective-permute-start.5 = (bf16[16,192,192]{2,1,0:T(8,128)(2,1)}, bf16[16,192,192]{2,1,0:T(8,128)(2,1)}, u32[]{:S(2)}, u32[]{:S(2)}) collective-permute-start(bf16[16,192,192]{2,1,0:T(8,128)(2,1)} %get-tuple-element.42), channel_id=1, source_target_pairs={{1,0},{2,1},{3,2},{4,3},{5,4},{6,5},{7,6},{8,7},{9,8},{10,9},{11,1... | collective-permute-start | bytes 3538952 | tf_op jit(solution)/shard_map/ppermute | solution.py:30
  553.0 24.3 %collective-permute-start.10 = (bf16[16,192,192]{2,1,0:T(8,128)(2,1)}, bf16[16,192,192]{2,1,0:T(8,128)(2,1)S(1)}, u32[]{:S(2)}, u32[]{:S(2)}) collective-permute-start(bf16[16,192,192]{2,1,0:T(8,128)(2,1)} %get-tuple-element.47), channel_id=1, source_target_pairs={{0,1},{1,2},{2,3},{3,4},{4,5},{5,6},{6,7},{7,8},{8,9},{9,10},{10,1... | collective-permute-start | bytes 3538952 | tf_op jit(solution)/shard_map/ppermute | solution.py:27
  553.0 24.3 %collective-permute-start.11 = (bf16[16,192,192]{2,1,0:T(8,128)(2,1)}, bf16[16,192,192]{2,1,0:T(8,128)(2,1)}, u32[]{:S(2)}, u32[]{:S(2)}) collective-permute-start(bf16[16,192,192]{2,1,0:T(8,128)(2,1)} %get-tuple-element.48), channel_id=1, source_target_pairs={{1,0},{2,1},{3,2},{4,3},{5,4},{6,5},{7,6},{8,7},{9,8},{10,9},{11,1... | collective-permute-start | bytes 3538952 | tf_op jit(solution)/shard_map/ppermute | solution.py:30
  562.7 8.7 %copy-start = (f32[16,672,192]{2,1,0:T(8,128)}, f32[16,672,192]{2,1,0:T(8,128)S(1)}, u32[]{:S(2)}) copy-start(f32[16,672,192]{2,1,0:T(8,128)S(1)} %maximum_convert_fusion.2) | copy-start | bytes 24772612
  580.6 6.9 %copy-start.1 = (f32[16,672,192]{2,1,0:T(8,128)}, f32[16,672,192]{2,1,0:T(8,128)S(1)}, u32[]{:S(2)}) copy-start(f32[16,672,192]{2,1,0:T(8,128)S(1)} %maximum_convert_fusion.5) | copy-start | bytes 24772612
  590.5 20.2 %copy-start.13 = (f32[8,288,192]{2,1,0:T(8,128)S(1)}, f32[8,288,192]{2,1,0:T(8,128)}, u32[]{:S(2)}) copy-start(f32[8,288,192]{2,1,0:T(8,128)} %copy-done.12) | copy-start | bytes 5308420
  613.7 20.0 %copy-start.11 = (f32[8,288,192]{2,1,0:T(8,128)S(1)}, f32[8,288,192]{2,1,0:T(8,128)}, u32[]{:S(2)}) copy-start(f32[8,288,192]{2,1,0:T(8,128)} %copy-done.10) | copy-start | bytes 5308420
Sparse Core Ops, SparseCore 0:
  32.0 88.7 all-reduce.3
where the time goes:
time: 649 us; the launch traced here: 645 us
  blocking collectives  285 us (44%)
  other arithmetic  157 us (24%)
  local copies, waits for them, and re-layouts  79.5 us (12%)
  waiting for transfers between devices  69.1 us (11%)
  starting transfers between devices  38.4 us (6%)
  between operations  15.5 us (2%)
    psum x1, blocking collectives, body(): totals = lax.psum(local_sums, 'domain')  285 us
    convert_element_type x4, other arithmetic, solve_block(): potential.astype(jnp.bfloat16)  75.7 us
    slice x12, local copies, waits for them, and re-layouts, row_sweep(): jnp.roll(centre, -1, 2)  58 us
    psum x1, waiting for transfers between devices, spread(): return lax.psum(block, axis)  43.5 us
    div x2, other arithmetic, row_sweep(): return (beside + coupling * source) / 6.0  40.2 us
    ppermute x6, starting transfers between devices, padded(): lax.ppermute(lax.slice_in_dim(block, 0, width, axis=dim), axis, backward)  38.3 us
    ppermute x6, waiting for transfers between devices, padded(): lax.ppermute(lax.slice_in_dim(block, block.shape[dim] - width, None, axis...  25.4 us
    convert_element_type x6, other arithmetic, solve_block(): padded(potential.astype(jnp.bfloat16), (('domain', 1),), GY)  22.4 us
  transfers between devices with their start and end apart: 13, of which 6 were waited for; matrix products, arithmetic and copies ran while one was open for 17% of the time, Pallas kernels for 0%

commit v1 on v0

--- a/solution.py
+++ b/solution.py
@@ -86,7 +86,7 @@
     for block_index in range(STEPS):
         partner = fetch_block(partner_pool, owners, block_index)
         density, local_sums = pair_products(partner, targets)
-        totals = lax.psum(local_sums, "domain")
+        totals = jnp.sum(lax.all_gather(local_sums, "domain"), axis=0)
         exchange = exchange - solve_block(
             partner, density, totals / cell_count, warm_start[block_index], first_row
         )

time: 649 us -> 687 us (1.059)
  blocking collectives: 285 us -> 325 us
    all_gather x0 -> x2, blocking collectives: none -> 325 us  [body(): totals = jnp.sum(lax.all_gather(local_sums, 'domain'), axis=0)]
    psum x1 -> x0, blocking collectives: 285 us -> none  [body(): totals = lax.psum(local_sums, 'domain')]
  transfers between devices with their start and end apart: 13 -> 13, of which waited for: 6 -> 6; matrix products, arithmetic and copies ran while one was open for 17% -> 16% of each run, Pallas kernels for 0% -> 0%
where the time goes in v1:
time: 687 us; the launch traced here: 683 us
  blocking collectives  325 us (47%)
  other arithmetic  156 us (23%)
  local copies, waits for them, and re-layouts  79.8 us (12%)
  waiting for transfers between devices  69.1 us (10%)
  starting transfers between devices  38.4 us (6%)
  between operations  15.1 us (2%)
    all_gather x2, blocking collectives, body(): totals = jnp.sum(lax.all_gather(local_sums, 'domain'), axis=0)  325 us
    convert_element_type x4, other arithmetic, solve_block(): potential.astype(jnp.bfloat16)  74.9 us
    slice x12, local copies, waits for them, and re-layouts, row_sweep(): jnp.roll(centre, -1, 2)  58.1 us
    psum x1, waiting for transfers between devices, spread(): return lax.psum(block, axis)  43.5 us
    div x2, other arithmetic, row_sweep(): return (beside + coupling * source) / 6.0  40.1 us
    ppermute x6, starting transfers between devices, padded(): lax.ppermute(lax.slice_in_dim(block, 0, width, axis=dim), axis, backward)  37.8 us
    ppermute x6, waiting for transfers between devices, padded(): lax.ppermute(lax.slice_in_dim(block, block.shape[dim] - width, None, axis...  25.4 us
    convert_element_type x6, other arithmetic, solve_block(): padded(potential.astype(jnp.bfloat16), (('domain', 1),), GY)  22.4 us
  transfers between devices with their start and end apart: 13, of which 6 were waited for; matrix products, arithmetic and copies ran while one was open for 16% of the time, Pallas kernels for 0%

profile of v1, /device:TPU:8, one launch (start us, length us, event | category | flops | bytes accessed | tf_op | source)
XLA Modules:
  0.0 683.5 jit_solution(17525781403238457589)
XLA Ops:
  11.4 7.4 %collective-permute-start.1 = (bf16[16,192,192]{2,1,0:T(8,128)(2,1)}, bf16[16,192,192]{2,1,0:T(8,128)(2,1)}, u32[]{:S(2)}, u32[]{:S(2)}) collective-permute-start(bf16[16,192,192]{2,1,0:T(8,128)(2,1)} %get-tuple-element.44), channel_id=1, source_target_pairs={{1,0},{2,1},{3,2},{4,3},{5,4},{6,5},{7,6},{8,7},{9,8},{10,9},{11,1... | collective-permute-start | bytes 3538952 | tf_op jit(solution)/shard_map/ppermute | solution.py:30
  20.3 6.5 collective-permute-start.7
  31.9 5.3 collective-permute-done
  37.2 4.5 maximum_convert_fusion
  45.2 8.9 %collective-permute-done.6 = bf16[16,192,192]{2,1,0:T(8,128)(2,1)} collective-permute-done((bf16[16,192,192]{2,1,0:T(8,128)(2,1)}, bf16[16,192,192]{2,1,0:T(8,128)(2,1)}, u32[]{:S(2)}, u32[]{:S(2)}) %collective-permute-start.6) | collective-permute-done | bytes 1179680 | tf_op jit(solution)/shard_map/ppermute | solution.py:27
  54.1 3.8 maximum_convert_fusion.3
  61.4 10.5 %fusion.51 = (f32[16,288,191]{2,1,0:T(8,128)}, f32[16,288,191]{2,1,0:T(8,128)}) fusion(f32[16,672,192]{2,1,0:T(8,128)} %copy-done.3), kind=kLoop, calls=%fused_computation.90 | loop fusion | bytes 14082048 | tf_op jit(solution)/shard_map/jit(_roll_static)/slice | solution.py:51
  71.9 5.4 fusion.57
  77.3 43.5 %all-reduce.3.cloned.1.call-done = (bf16[8,288,192]{2,1,0:T(8,128)(2,1)}, bf16[8,288,192]{2,1,0:T(8,128)(2,1)}) async-done(((bf16[8,288,192]{2,1,0:T(8,128)(2,1)}, bf16[8,288,192]{2,1,0:T(8,128)(2,1)}), (bf16[8,288,192]{2,1,0:T(8,128)(2,1)}, bf16[8,288,192]{2,1,0:T(8,128)(2,1)})) %all-reduce.3.cloned.1.call-update) | async-done | bytes 1769488 | tf_op jit(solution)/shard_map/psum | solution.py:18
  124.7 4.9 fusion.42
  129.7 157.3 %all-gather.2 = f32[128,8,2]{1,2,0:T(2,128)S(1)} all-gather(f32[1,8,2]{1,2,0:T(2,128)S(1)} %bitcast.34), channel_id=2, replica_groups=mesh['band'=2,'domain'=128] {'domain'}, dimensions={0}, use_global_device_ids=true | all-gather | bytes 8256 | tf_op jit(solution)/shard_map/all_gather | solution.py:89
  287.3 17.9 %fusion.38 = bf16[16,288,192]{2,1,0:T(8,128)(2,1)S(1)} fusion(f32[16,672,192]{2,1,0:T(8,128)} %copy-done.3, f32[16,288,191]{2,1,0:T(8,128)} %get-tuple-element.18, f32[16,288,1]{2,1,0:T(8,128)} %get-tuple-element.20, f32[16,288,1]{2,1,0:T(8,128)} %get-tuple-element.19, f32[16,288,191]{2,1,0:T(8,128)} %get-tuple-element.17, ...), kind=kLoop, calls=%fused_computation.60 | loop fusion | flops 12386304 | bytes 33620608 | tf_op jit(solution)/shard_map/convert_element_type | solution.py:73
  307.7 5.6 collective-permute-start.3
  313.4 167.2 %all-gather.3 = f32[128,8,2]{1,2,0:T(2,128)S(1)} all-gather(f32[1,8,2]{1,2,0:T(2,128)S(1)} %bitcast.35), channel_id=3, replica_groups=mesh['band'=2,'domain'=128] {'domain'}, dimensions={0}, use_global_device_ids=true | all-gather | bytes 8256 | tf_op jit(solution)/shard_map/all_gather | solution.py:89
  480.9 19.5 %fusion.18 = bf16[16,288,192]{2,1,0:T(8,128)(2,1)} fusion(f32[16,672,192]{2,1,0:T(8,128)} %copy-done.2, f32[16,288,191]{2,1,0:T(8,128)} %get-tuple-element.30, f32[16,288,1]{2,1,0:T(8,128)} %get-tuple-element.32, f32[16,288,1]{2,1,0:T(8,128)} %get-tuple-element.31, f32[16,288,191]{2,1,0:T(8,128)} %get-tuple-element.29, ...), kind=kLoop, calls=%fused_computation.31 | loop fusion | flops 12386304 | bytes 33620608 | tf_op jit(solution)/shard_map/convert_element_type | solution.py:73
  500.5 3.8 fusion.64
  504.6 5.8 collective-permute-start.9
  510.5 3.8 maximum_convert_fusion.1
  517.9 5.3 fusion.49
  523.2 5.4 collective-permute-done.8
  532.0 5.8 fusion.55
  541.9 18.0 %fusion.31 = bf16[16,288,192]{2,1,0:T(8,128)(2,1)S(1)} fusion(f32[16,672,192]{2,1,0:T(8,128)} %copy-done.5, f32[16,288,191]{2,1,0:T(8,128)} %get-tuple-element.14, f32[16,288,1]{2,1,0:T(8,128)} %get-tuple-element.16, f32[16,288,1]{2,1,0:T(8,128)} %get-tuple-element.15, f32[16,288,191]{2,1,0:T(8,128)} %get-tuple-element.13, ...), kind=kLoop, calls=%fused_computation.50 | loop fusion | flops 12386304 | bytes 33620608 | tf_op jit(solution)/shard_map/convert_element_type | solution.py:73
  562.1 6.5 collective-permute-start.5
  568.6 19.5 %fusion.11 = bf16[16,288,192]{2,1,0:T(8,128)(2,1)} fusion(f32[16,672,192]{2,1,0:T(8,128)} %copy-done.4, f32[16,288,191]{2,1,0:T(8,128)} %get-tuple-element.26, f32[16,288,1]{2,1,0:T(8,128)} %get-tuple-element.28, f32[16,288,1]{2,1,0:T(8,128)} %get-tuple-element.27, f32[16,288,191]{2,1,0:T(8,128)} %get-tuple-element.25, ...), kind=kLoop, calls=%fused_computation.21 | loop fusion | flops 12386304 | bytes 33620608 | tf_op jit(solution)/shard_map/convert_element_type | solution.py:73
  588.1 3.9 fusion.63
  592.0 6.0 collective-permute-start.11
  597.9 3.8 maximum_convert_fusion.2
  605.0 5.3 fusion.47
  610.4 5.9 collective-permute-done.10
  619.6 5.8 fusion.53
  629.5 20.2 %fusion.24 = f32[16,288,192]{2,1,0:T(8,128)} fusion(f32[16,672,192]{2,1,0:T(8,128)} %copy-done, f32[16,288,191]{2,1,0:T(8,128)} %get-tuple-element.10, f32[16,288,1]{2,1,0:T(8,128)} %get-tuple-element.12, f32[16,288,1]{2,1,0:T(8,128)} %get-tuple-element.11, f32[16,288,191]{2,1,0:T(8,128)} %get-tuple-element.9, f32[8,2,288,192]{3,2,1,0:T(8,128)} %get-tuple-element.37, ...), kind=kLoop, calls=%fused_computation.40 | loop fusion | flops 11501568 | bytes 35390080 | tf_op jit(solution)/shard_map/div | solution.py:52
  652.6 19.9 %fusion.4 = f32[16,288,192]{2,1,0:T(8,128)} fusion(f32[16,672,192]{2,1,0:T(8,128)} %copy-done.1, f32[16,288,191]{2,1,0:T(8,128)} %get-tuple-element.22, f32[16,288,1]{2,1,0:T(8,128)} %get-tuple-element.24, f32[16,288,1]{2,1,0:T(8,128)} %get-tuple-element.23, f32[16,288,191]{2,1,0:T(8,128)} %get-tuple-element.21, f32[8,2,288,192]{3,2,1,0:T(8,128)} %get-tuple-element.38, ...), kind=kLoop, calls=%fused_computation.11 | loop fusion | flops 11501568 | bytes 35390080 | tf_op jit(solution)/shard_map/div | solution.py:52
  (79 shorter events, 55.5 us)
Async XLA Ops:
  6.5 114.3 %all-reduce.3.cloned.1.call-start = ((), (), s32[]{:S(2)}) async-start(), calls=%async_computation | async-start | bytes 4718592 | tf_op jit(solution)/shard_map/psum | solution.py:18
  9.2 11.0 %copy-start.8 = (bf16[1,8,2,288,192]{4,3,2,1,0:T(8,128)(2,1)}, bf16[1,8,2,288,192]{4,3,2,1,0:T(8,128)(2,1)S(1)}, u32[]{:S(2)}) copy-start(bf16[1,8,2,288,192]{4,3,2,1,0:T(8,128)(2,1)S(1)} %get-tuple-element.34) | copy-start | bytes 5308420
  9.2 11.0 %copy-start.9 = (bf16[1,8,2,288,192]{4,3,2,1,0:T(8,128)(2,1)}, bf16[1,8,2,288,192]{4,3,2,1,0:T(8,128)(2,1)S(1)}, u32[]{:S(2)}) copy-start(bf16[1,8,2,288,192]{4,3,2,1,0:T(8,128)(2,1)S(1)} %get-tuple-element.33) | copy-start | bytes 5308420
  11.4 15.4 %copy-start.15 = (s32[2]{0:T(128)S(1)}, s32[2]{0:T(128)}, u32[]{:S(2)}) copy-start(s32[2]{0:T(128)} %param.6) | copy-start | bytes 28
  11.4 25.8 %collective-permute-start = (bf16[16,192,192]{2,1,0:T(8,128)(2,1)}, bf16[16,192,192]{2,1,0:T(8,128)(2,1)}, u32[]{:S(2)}, u32[]{:S(2)}) collective-permute-start(bf16[16,192,192]{2,1,0:T(8,128)(2,1)} %get-tuple-element.43), channel_id=1, source_target_pairs={{0,1},{1,2},{2,3},{3,4},{4,5},{5,6},{6,7},{7,8},{8,9},{9,10},{10,1... | collective-permute-start | bytes 3538952 | tf_op jit(solution)/shard_map/ppermute | solution.py:27
  11.4 25.8 %collective-permute-start.1 = (bf16[16,192,192]{2,1,0:T(8,128)(2,1)}, bf16[16,192,192]{2,1,0:T(8,128)(2,1)}, u32[]{:S(2)}, u32[]{:S(2)}) collective-permute-start(bf16[16,192,192]{2,1,0:T(8,128)(2,1)} %get-tuple-element.44), channel_id=1, source_target_pairs={{1,0},{2,1},{3,2},{4,3},{5,4},{6,5},{7,6},{8,7},{9,8},{10,9},{11,1... | collective-permute-start | bytes 3538952 | tf_op jit(solution)/shard_map/ppermute | solution.py:30
  20.3 33.9 %collective-permute-start.6 = (bf16[16,192,192]{2,1,0:T(8,128)(2,1)}, bf16[16,192,192]{2,1,0:T(8,128)(2,1)}, u32[]{:S(2)}, u32[]{:S(2)}) collective-permute-start(bf16[16,192,192]{2,1,0:T(8,128)(2,1)} %get-tuple-element.49), channel_id=1, source_target_pairs={{0,1},{1,2},{2,3},{3,4},{4,5},{5,6},{6,7},{7,8},{8,9},{9,10},{10,1... | collective-permute-start | bytes 3538952 | tf_op jit(solution)/shard_map/ppermute | solution.py:27
  20.3 33.9 %collective-permute-start.7 = (bf16[16,192,192]{2,1,0:T(8,128)(2,1)S(1)}, bf16[16,192,192]{2,1,0:T(8,128)(2,1)}, u32[]{:S(2)}, u32[]{:S(2)}) collective-permute-start(bf16[16,192,192]{2,1,0:T(8,128)(2,1)S(1)} %get-tuple-element.50), channel_id=1, source_target_pairs={{1,0},{2,1},{3,2},{4,3},{5,4},{6,5},{7,6},{8,7},{9,8},{10,9},{11,1... | collective-permute-start | bytes 3538952 | tf_op jit(solution)/shard_map/ppermute | solution.py:30
  41.7 12.4 %copy-start.3 = (f32[16,672,192]{2,1,0:T(8,128)}, f32[16,672,192]{2,1,0:T(8,128)S(1)}, u32[]{:S(2)}) copy-start(f32[16,672,192]{2,1,0:T(8,128)S(1)} %maximum_convert_fusion) | copy-start | bytes 24772612
  57.9 14.0 %copy-start.2 = (f32[16,672,192]{2,1,0:T(8,128)}, f32[16,672,192]{2,1,0:T(8,128)S(1)}, u32[]{:S(2)}) copy-start(f32[16,672,192]{2,1,0:T(8,128)S(1)} %maximum_convert_fusion.3) | copy-start | bytes 24772612
  77.3 47.4 %copy-start.14 = (f32[2,288,192]{2,1,0:T(8,128)S(1)}, f32[2,288,192]{2,1,0:T(8,128)}, u32[]{:S(2)}) copy-start(f32[2,288,192]{2,1,0:T(8,128)} %param.4) | copy-start | bytes 1327108
  122.3 7.2 %copy-start.12 = (f32[8,288,192]{2,1,0:T(8,128)}, f32[8,288,192]{2,1,0:T(8,128)S(1)}, u32[]{:S(2)}) copy-start(f32[8,288,192]{2,1,0:T(8,128)S(1)} %convert_element_type.41) | copy-start | bytes 5308420
  124.7 4.9 copy-start.10
  305.2 195.2 %copy-start.6 = (bf16[16,288,192]{2,1,0:T(8,128)(2,1)}, bf16[16,288,192]{2,1,0:T(8,128)(2,1)S(1)}, u32[]{:S(2)}) copy-start(bf16[16,288,192]{2,1,0:T(8,128)(2,1)S(1)} %fusion.38) | copy-start | bytes 5308420
  307.4 203.1 %collective-permute-start.2 = (bf16[16,192,192]{2,1,0:T(8,128)(2,1)}, bf16[16,192,192]{2,1,0:T(8,128)(2,1)}, u32[]{:S(2)}, u32[]{:S(2)}) collective-permute-start(bf16[16,192,192]{2,1,0:T(8,128)(2,1)} %get-tuple-element.41), channel_id=1, source_target_pairs={{0,1},{1,2},{2,3},{3,4},{4,5},{5,6},{6,7},{7,8},{8,9},{9,10},{10,1... | collective-permute-start | bytes 3538952 | tf_op jit(solution)/shard_map/ppermute | solution.py:27
  307.7 202.8 %collective-permute-start.3 = (bf16[16,192,192]{2,1,0:T(8,128)(2,1)}, bf16[16,192,192]{2,1,0:T(8,128)(2,1)}, u32[]{:S(2)}, u32[]{:S(2)}) collective-permute-start(bf16[16,192,192]{2,1,0:T(8,128)(2,1)} %get-tuple-element.42), channel_id=1, source_target_pairs={{1,0},{2,1},{3,2},{4,3},{5,4},{6,5},{7,6},{8,7},{9,8},{10,9},{11,1... | collective-permute-start | bytes 3538952 | tf_op jit(solution)/shard_map/ppermute | solution.py:30
  504.3 24.3 %collective-permute-start.8 = (bf16[16,192,192]{2,1,0:T(8,128)(2,1)}, bf16[16,192,192]{2,1,0:T(8,128)(2,1)S(1)}, u32[]{:S(2)}, u32[]{:S(2)}) collective-permute-start(bf16[16,192,192]{2,1,0:T(8,128)(2,1)} %get-tuple-element.47), channel_id=1, source_target_pairs={{0,1},{1,2},{2,3},{3,4},{4,5},{5,6},{6,7},{7,8},{8,9},{9,10},{10,1... | collective-permute-start | bytes 3538952 | tf_op jit(solution)/shard_map/ppermute | solution.py:27
  504.6 24.1 %collective-permute-start.9 = (bf16[16,192,192]{2,1,0:T(8,128)(2,1)}, bf16[16,192,192]{2,1,0:T(8,128)(2,1)}, u32[]{:S(2)}, u32[]{:S(2)}) collective-permute-start(bf16[16,192,192]{2,1,0:T(8,128)(2,1)} %get-tuple-element.48), channel_id=1, source_target_pairs={{1,0},{2,1},{3,2},{4,3},{5,4},{6,5},{7,6},{8,7},{9,8},{10,9},{11,1... | collective-permute-start | bytes 3538952 | tf_op jit(solution)/shard_map/ppermute | solution.py:30
  514.2 9.0 %copy-start.5 = (f32[16,672,192]{2,1,0:T(8,128)}, f32[16,672,192]{2,1,0:T(8,128)S(1)}, u32[]{:S(2)}) copy-start(f32[16,672,192]{2,1,0:T(8,128)S(1)} %maximum_convert_fusion.1) | copy-start | bytes 24772612
  532.0 6.9 %copy-start.4 = (f32[16,672,192]{2,1,0:T(8,128)}, f32[16,672,192]{2,1,0:T(8,128)S(1)}, u32[]{:S(2)}) copy-start(f32[16,672,192]{2,1,0:T(8,128)S(1)} %maximum_convert_fusion.4) | copy-start | bytes 24772612
  559.9 28.2 %copy-start.7 = (bf16[16,288,192]{2,1,0:T(8,128)(2,1)}, bf16[16,288,192]{2,1,0:T(8,128)(2,1)S(1)}, u32[]{:S(2)}) copy-start(bf16[16,288,192]{2,1,0:T(8,128)(2,1)S(1)} %fusion.31) | copy-start | bytes 5308420
  562.1 35.9 %collective-permute-start.4 = (bf16[16,192,192]{2,1,0:T(8,128)(2,1)}, bf16[16,192,192]{2,1,0:T(8,128)(2,1)}, u32[]{:S(2)}, u32[]{:S(2)}) collective-permute-start(bf16[16,192,192]{2,1,0:T(8,128)(2,1)} %get-tuple-element.39), channel_id=1, source_target_pairs={{0,1},{1,2},{2,3},{3,4},{4,5},{5,6},{6,7},{7,8},{8,9},{9,10},{10,1... | collective-permute-start | bytes 3538952 | tf_op jit(solution)/shard_map/ppermute | solution.py:27
  562.1 35.9 %collective-permute-start.5 = (bf16[16,192,192]{2,1,0:T(8,128)(2,1)}, bf16[16,192,192]{2,1,0:T(8,128)(2,1)}, u32[]{:S(2)}, u32[]{:S(2)}) collective-permute-start(bf16[16,192,192]{2,1,0:T(8,128)(2,1)} %get-tuple-element.40), channel_id=1, source_target_pairs={{1,0},{2,1},{3,2},{4,3},{5,4},{6,5},{7,6},{8,7},{9,8},{10,9},{11,1... | collective-permute-start | bytes 3538952 | tf_op jit(solution)/shard_map/ppermute | solution.py:30
  592.0 24.3 %collective-permute-start.10 = (bf16[16,192,192]{2,1,0:T(8,128)(2,1)}, bf16[16,192,192]{2,1,0:T(8,128)(2,1)S(1)}, u32[]{:S(2)}, u32[]{:S(2)}) collective-permute-start(bf16[16,192,192]{2,1,0:T(8,128)(2,1)} %get-tuple-element.45), channel_id=1, source_target_pairs={{0,1},{1,2},{2,3},{3,4},{4,5},{5,6},{6,7},{7,8},{8,9},{9,10},{10,1... | collective-permute-start | bytes 3538952 | tf_op jit(solution)/shard_map/ppermute | solution.py:27
  592.0 24.3 %collective-permute-start.11 = (bf16[16,192,192]{2,1,0:T(8,128)(2,1)}, bf16[16,192,192]{2,1,0:T(8,128)(2,1)}, u32[]{:S(2)}, u32[]{:S(2)}) collective-permute-start(bf16[16,192,192]{2,1,0:T(8,128)(2,1)} %get-tuple-element.46), channel_id=1, source_target_pairs={{1,0},{2,1},{3,2},{4,3},{5,4},{6,5},{7,6},{8,7},{9,8},{10,9},{11,1... | collective-permute-start | bytes 3538952 | tf_op jit(solution)/shard_map/ppermute | solution.py:30
  601.7 8.7 %copy-start = (f32[16,672,192]{2,1,0:T(8,128)}, f32[16,672,192]{2,1,0:T(8,128)S(1)}, u32[]{:S(2)}) copy-start(f32[16,672,192]{2,1,0:T(8,128)S(1)} %maximum_convert_fusion.2) | copy-start | bytes 24772612
  619.6 6.9 %copy-start.1 = (f32[16,672,192]{2,1,0:T(8,128)}, f32[16,672,192]{2,1,0:T(8,128)S(1)}, u32[]{:S(2)}) copy-start(f32[16,672,192]{2,1,0:T(8,128)S(1)} %maximum_convert_fusion.5) | copy-start | bytes 24772612
  629.5 20.2 %copy-start.13 = (f32[8,288,192]{2,1,0:T(8,128)S(1)}, f32[8,288,192]{2,1,0:T(8,128)}, u32[]{:S(2)}) copy-start(f32[8,288,192]{2,1,0:T(8,128)} %copy-done.12) | copy-start | bytes 5308420
  652.6 20.0 %copy-start.11 = (f32[8,288,192]{2,1,0:T(8,128)S(1)}, f32[8,288,192]{2,1,0:T(8,128)}, u32[]{:S(2)}) copy-start(f32[8,288,192]{2,1,0:T(8,128)} %copy-done.10) | copy-start | bytes 5308420
Sparse Core Ops, SparseCore 0:
  32.0 88.8 all-reduce.2
